TPU v7x, 512 devices: a whole 4x8x8 slice. The times are simulated.
512 devices in a mesh: band: 32 (over x, y), seq: 16 (over z, core).
Axes of the slice: x: 4, y: 8, z: 8, core: 2. Of those that a mesh axis runs over, the one named last changes fastest.
Arguments:
- posteriors: bfloat16 [32, 262144], P(None, ('band', 'seq'))
- seed_mask: int32 [262144], P(('band', 'seq')), may hold values 0 or 1
- frame_perm: int32 [512, 512], P(('band', 'seq')), may hold values from 0 to 511, each once within a row
- lengths: int32 [256], replicated, may hold values from 1 to 4096, 262144 in all
- embeddings: bfloat16 [262144, 256], P(('band', 'seq')), may hold values from -12 to 12
- partners: int32 [2048, 32], P(('band', 'seq')), may hold values from 0 to 127, as said below
- levels: int32 [2048, 32], P(('band', 'seq')), may hold values from 1 to 8, as said below
Outputs:
- spread_labels: float32 [32, 262144], P(None, ('band', 'seq'))
Inputs may be any that keep to these rules, and one draw needn't show every extreme that they name: `partners`: within each seq index s, slot k pairs the 128 tiles mutually: if tile number a names b in slot k then b names a in slot k; no tile names itself. `levels`: two tiles paired in slot k carry the same level.
All inputs are finite; a program needn't handle non-finite values. No bound on the sum of `seed_mask` on one device may be relied on, other than what follows from the above.
Results may differ from a plain program's by a relative error of at most 0.007.
Values may be sent and summed in bfloat16 or wider, within the bound.
No kernel may reach another device: no remote copies, remote signals or barrier semaphores. Data moves between devices by JAX's collectives and lax.ppermute only.
A program may use at most 64 MiB of HBM per device.

v0:
```python
import math
import jax
import jax.numpy as jnp
from jax import lax
from jax.sharding import PartitionSpec as P

RADIUS = 64
ITERS = 3
decay_len = 16.0
spread_rate = 0.9


def with_halo(cells, sides, width):
    for axis, dim in sides:
        count = lax.axis_size(axis)
        ends = count - 1
        head = lax.slice_in_dim(cells, 0, width, axis=dim)
        tail = lax.slice_in_dim(cells, cells.shape[dim] - width, cells.shape[dim], axis=dim)
        cells = jnp.concatenate(
            [
                lax.ppermute(tail, axis, [(i, (i + 1) % count) for i in range(ends)]),
                cells,
                lax.ppermute(head, axis, [((i + 1) % count, i) for i in range(ends)]),
            ],
            axis=dim,
        )
    return cells


def on_device(posteriors, seed_mask, frame_perm, lengths, embeddings, partners, levels):
    channels, frames = posteriors.shape
    band_count = lax.axis_size("band")
    groups = lax.axis_size("seq")
    tile_count = frames // 128
    seeded = posteriors * seed_mask.astype(jnp.bfloat16)[None, :]
    ordered = jnp.take(seeded, frame_perm[0], axis=1).reshape(
        channels, band_count, frames // band_count
    )
    arrived = lax.all_to_all(ordered, "band", split_axis=1, concat_axis=1, tiled=True)
    labels = arrived.reshape(channels, frames).astype(jnp.float32)
    device = lax.axis_index("band") * groups + lax.axis_index("seq")
    frame_total = frames * band_count * groups
    window = 128 + 2 * RADIUS
    global_at = device * frames - RADIUS + jnp.arange(frames + 2 * RADIUS, dtype=jnp.int32)
    utt_ends = jnp.cumsum(lengths)
    owner_seg = jnp.sum((utt_ends[None, :] <= global_at[:, None]).astype(jnp.int32), axis=1)
    inside = (global_at >= 0) & (global_at < frame_total)
    tile_off = (jnp.arange(tile_count, dtype=jnp.int32) * 128)[:, None, None]
    win_pos = tile_off + jnp.arange(window, dtype=jnp.int32)[None, :, None]
    row_pos = tile_off + RADIUS + jnp.arange(128, dtype=jnp.int32)[None, None, :]
    offset = jnp.abs(win_pos - row_pos)
    linked = (
        (offset >= 1)
        & (offset <= RADIUS)
        & (owner_seg[win_pos] == owner_seg[row_pos])
        & inside[win_pos]
    )
    band_tiles = jnp.where(
        linked, jnp.exp(-offset.astype(jnp.float32) / decay_len), jnp.float32(0.0)
    ).astype(jnp.bfloat16)
    near_degree = jnp.sum(band_tiles.astype(jnp.float32), axis=1).reshape(frames)
    gathered = lax.all_gather(embeddings, "band", axis=0, tiled=True)
    embed_width = embeddings.shape[1]
    partner_rows = gathered.reshape(-1, 128, embed_width)[partners]
    own_rows = embeddings.reshape(tile_count, 128, embed_width)
    inner_prod = jnp.einsum(
        "tkje,tie->tkji", partner_rows, own_rows, preferred_element_type=jnp.float32
    )
    affinity = (
        jnp.exp(0.5 * (inner_prod / math.sqrt(embed_width)))
        * (levels.astype(jnp.float32) / 8.0)[:, :, None, None]
        / 128.0
    )
    affinity = affinity.astype(jnp.bfloat16)
    far_degree = jnp.sum(affinity.astype(jnp.float32), axis=(1, 2)).reshape(frames)
    norm_scale = 1.0 / jnp.sqrt(near_degree + far_degree)

    def squares(residual):
        return lax.psum(jnp.sum(residual * residual, axis=1), ("band", "seq"))

    solution = jnp.zeros((channels, frames), jnp.float32)
    residual = labels
    direction = labels
    norm_now = squares(residual)
    for iteration in range(ITERS):
        lifted = (norm_scale[None, :] * direction).astype(jnp.bfloat16)
        padded = with_halo(lifted, ((("band", "seq"), 1),), RADIUS)
        windows = jnp.stack(
            [padded[:, position * 128 : position * 128 + window] for position in range(tile_count)],
            axis=0,
        )
        near_term = jnp.einsum(
            "tcw,twa->cta", windows, band_tiles, preferred_element_type=jnp.float32
        ).reshape(channels, frames)
        spread = lax.all_gather(lifted, "band", axis=1, tiled=True).reshape(channels, -1, 128)
        far_tiles = spread[:, partners]
        far_term = jnp.einsum(
            "ctkj,tkji->cti", far_tiles, affinity, preferred_element_type=jnp.float32
        ).reshape(channels, frames)
        image = direction - spread_rate * norm_scale[None, :] * (near_term + far_term)
        curve = lax.psum(jnp.sum(direction * image, axis=1), ("band", "seq"))
        alpha = norm_now / curve
        solution = solution + alpha[:, None] * direction
        residual = residual - alpha[:, None] * image
        norm_next = squares(residual)
        direction = residual + (norm_next / norm_now)[:, None] * direction
        norm_now = norm_next
    return solution


def solution(mesh):
    placed = (
        P(None, ("band", "seq")),
        P(("band", "seq")),
        P(("band", "seq"), None),
        P(),
        P(("band", "seq"), None),
        P(("band", "seq"), None),
        P(("band", "seq"), None),
    )
    return jax.shard_map(
        on_device, mesh=mesh, in_specs=placed, out_specs=P(None, ("band", "seq")), check_vma=False
    )
```

profile of v0, /device:TPU:1, one launch (start us, length us, event | category | flops | bytes accessed | tf_op | source)
XLA Modules:
  0.0 862.8 jit_solution(14141777168958132764)
XLA Ops:
  6.5 0.7 all-gather.5.cloned.1.call-update
  7.3 0.7 convert_element_type.47
  7.9 0.8 broadcast_multiply_fusion
  8.8 0.5 broadcast.328
  9.4 1.3 reduce.11
  10.8 0.7 compare_select_fusion.1
  11.5 1.3 gather_fusion
  12.8 0.1 fusion.73
  13.0 0.8 reshape.489
  13.7 10.5 %all-to-all-start = ((bf16[32,2,256]{2,1,0:T(2,128)(2,1)}), bf16[32,2,256]{2,1,0:T(2,128)(2,1)S(1)}, u32[]{:S(2)}, u32[]{:S(2)}) async-start(bf16[32,2,256]{2,1,0:T(2,128)(2,1)} %reshape.489), calls=%async_computation | async-start | bytes 65536 | tf_op jit(solution)/shard_map/all_to_all | solution.py:39
  24.3 1.0 reduce-window.9
  25.7 0.3 convert_reduce_fusion.1
  26.0 4.5 gather_fusion.1
  30.6 2.3 gather_fusion.2
  32.9 6.8 gather_fusion.3
  40.0 0.6 convert_reduce_fusion.2
  40.8 78.1 %all-gather.5.cloned.1.call-done = bf16[16384,256]{1,0:T(8,128)(2,1)} async-done(((bf16[512,256]{1,0:T(8,128)(2,1)}), bf16[16384,256]{1,0:T(8,128)(2,1)}) %all-gather.5.cloned.1.call-update) | async-done | bytes 8388624 | tf_op jit(solution)/shard_map/all_gather | solution.py:62
  118.9 10.0 %gather_fusion.4 = bf16[128,128,256]{2,1,0:T(8,128)(2,1)} fusion(bf16[128,128,256]{2,1,0:T(8,128)(2,1)} %bitcast.161, s32[1024]{0:T(1024)S(1)} %pad_clamp_fusion), kind=kCustom, calls=%fused_computation.4 | custom fusion | bytes 16777728 | tf_op jit(solution)/shard_map/gather | solution.py:64
  128.9 7.7 convert_reduce_fusion
  136.6 0.6 multiply_convert_fusion.3
  137.3 0.8 fusion.72
  138.1 4.2 collective-permute-start
  142.4 1.9 collective-permute-start.1
  144.4 2.9 collective-permute-done.1
  147.3 0.9 fusion.49
  148.3 0.6 fusion.13
  148.9 58.6 %all-gather.7.cloned.1.call-done = bf16[32,16384]{1,0:T(8,128)(2,1)} async-done(((bf16[32,512]{1,0:T(8,128)(2,1)}), bf16[32,16384]{1,0:T(8,128)(2,1)}) %all-gather.7.cloned.1.call-update) | async-done | bytes 1048592 | tf_op jit(solution)/shard_map/all_gather | solution.py:95
  207.5 1.4 copy_bitcast_fusion.2
  208.9 0.8 gather_fusion.5
  209.7 2.9 fusion.3
  212.8 0.2 fusion.10
  212.9 102.0 %all-reduce = (f32[32]{0:T(128)S(1)}, f32[32]{0:T(128)S(1)}) all-reduce(f32[32]{0:T(128)S(1)} %get-tuple-element.6, f32[32]{0:T(128)S(1)} %get-tuple-element.5), channel_id=1, replica_groups=mesh['band'=32,'seq'=16] {'band','seq'}, use_global_device_ids=true, to_apply=%region_1.2 | all-reduce | flops 64 | bytes 512 | tf_op jit(solution)/shard_map/psum | solution.py:79
  315.0 0.2 multiply_reduce_fusion.2
  315.1 94.4 %psum.44 = f32[32]{0:T(128)S(1)} all-reduce(f32[32]{0:T(128)S(1)} %multiply_reduce_fusion.2), channel_id=1, replica_groups=mesh['band'=32,'seq'=16] {'band','seq'}, use_global_device_ids=true, to_apply=%region_10.11 | all-reduce | flops 32 | bytes 256 | tf_op jit(solution)/shard_map/psum | solution.py:79
  409.5 0.7 multiply_convert_fusion.2
  410.3 0.8 fusion.71
  411.1 3.1 collective-permute-start.2
  414.2 2.1 collective-permute-start.3
  416.3 2.9 collective-permute-done.3
  419.1 0.9 fusion.47
  420.1 0.6 fusion.14
  420.7 57.0 %all-gather.9.cloned.1.call-done = bf16[32,16384]{1,0:T(8,128)(2,1)} async-done(((bf16[32,512]{1,0:T(8,128)(2,1)}), bf16[32,16384]{1,0:T(8,128)(2,1)}) %all-gather.9.cloned.1.call-update) | async-done | bytes 1048592 | tf_op jit(solution)/shard_map/all_gather | solution.py:95
  477.7 1.4 copy_bitcast_fusion.1
  479.1 0.8 gather_fusion.6
  479.9 2.9 fusion.2
  482.8 0.1 copy.53
  482.9 0.2 multiply_reduce_fusion.1
  483.1 102.0 %psum.45 = f32[32]{0:T(128)S(1)} all-reduce(f32[32]{0:T(128)S(1)} %multiply_reduce_fusion.1), channel_id=1, replica_groups=mesh['band'=32,'seq'=16] {'band','seq'}, use_global_device_ids=true, to_apply=%region_12.13 | all-reduce | flops 32 | bytes 256 | tf_op jit(solution)/shard_map/psum | solution.py:101
  585.2 0.2 multiply_reduce_fusion
  585.4 94.4 %psum.46 = f32[32]{0:T(128)S(1)} all-reduce(f32[32]{0:T(128)S(1)} %multiply_reduce_fusion), channel_id=1, replica_groups=mesh['band'=32,'seq'=16] {'band','seq'}, use_global_device_ids=true, to_apply=%region_14.15 | all-reduce | flops 32 | bytes 256 | tf_op jit(solution)/shard_map/psum | solution.py:79
  679.8 0.7 multiply_convert_fusion.1
  680.5 0.8 fusion.70
  681.3 3.1 collective-permute-start.4
  684.4 1.9 collective-permute-start.5
  686.3 3.0 collective-permute-done.5
  689.3 0.9 fusion.45
  690.3 0.6 fusion.15
  690.9 57.1 %all-gather.11.cloned.1.call-done = bf16[32,16384]{1,0:T(8,128)(2,1)} async-done(((bf16[32,512]{1,0:T(8,128)(2,1)}), bf16[32,16384]{1,0:T(8,128)(2,1)}) %all-gather.11.cloned.1.call-update) | async-done | bytes 1048592 | tf_op jit(solution)/shard_map/all_gather | solution.py:95
  748.0 1.4 copy_bitcast_fusion
  749.4 0.8 gather_fusion.7
  750.1 2.9 fusion.1
  753.2 0.2 fusion.12
  753.5 102.0 %psum.47 = f32[32]{0:T(128)S(1)} all-reduce(f32[32]{0:T(128)S(1)} %fusion.12), channel_id=1, replica_groups=mesh['band'=32,'seq'=16] {'band','seq'}, use_global_device_ids=true, to_apply=%region_16.17 | all-reduce | flops 32 | bytes 256 | tf_op jit(solution)/shard_map/psum | solution.py:101
  855.5 0.7 multiply_add_fusion
  (54 shorter events, 1.7 us)
Async XLA Ops:
  6.5 33.2 %copy-start.1 = (s32[4,32]{1,0:T(4,128)S(1)}, s32[4,32]{1,0:T(4,128)}, u32[]{:S(2)}) copy-start(s32[4,32]{1,0:T(4,128)} %param.12) | copy-start | bytes 1540
  6.5 34.0 %copy-start.2 = (s32[4,32]{1,0:T(4,128)S(1)}, s32[4,32]{1,0:T(4,128)}, u32[]{:S(2)}) copy-start(s32[4,32]{1,0:T(4,128)} %param.13) | copy-start | bytes 1540
  6.5 112.4 %all-gather.5.cloned.1.call-start = ((), (), s32[]{:S(2)}) async-start(), calls=%async_computation.1 | async-start | bytes 8650752 | tf_op jit(solution)/shard_map/all_gather | solution.py:62
  13.7 26.9 %all-to-all-start = ((bf16[32,2,256]{2,1,0:T(2,128)(2,1)}), bf16[32,2,256]{2,1,0:T(2,128)(2,1)S(1)}, u32[]{:S(2)}, u32[]{:S(2)}) async-start(bf16[32,2,256]{2,1,0:T(2,128)(2,1)} %reshape.489), calls=%async_computation | async-start | bytes 65536 | tf_op jit(solution)/shard_map/all_to_all | solution.py:39
  24.3 183.2 %all-gather.7.cloned.1.call-start = ((), (), s32[]{:S(2)}) async-start(), calls=%async_computation.2 | async-start | bytes 1081344 | tf_op jit(solution)/shard_map/all_gather | solution.py:95
  118.9 10.0 %copy-start = (bf16[512,256]{1,0:T(8,128)(2,1)S(1)}, bf16[512,256]{1,0:T(8,128)(2,1)}, u32[]{:S(2)}) copy-start(bf16[512,256]{1,0:T(8,128)(2,1)} %param.11) | copy-start | bytes 786436
  137.3 340.4 %all-gather.9.cloned.1.call-start = ((), (), s32[]{:S(2)}) async-start(), calls=%async_computation.3 | async-start | bytes 1081344 | tf_op jit(solution)/shard_map/all_gather | solution.py:95
  138.1 6.3 collective-permute-start
  142.4 5.0 collective-permute-start.1
  410.2 337.7 %all-gather.11.cloned.1.call-start = ((), (), s32[]{:S(2)}) async-start(), calls=%async_computation.4 | async-start | bytes 1081344 | tf_op jit(solution)/shard_map/all_gather | solution.py:95
  411.1 5.2 collective-permute-start.2
  414.2 5.0 collective-permute-start.3
  681.3 5.0 collective-permute-start.4
  684.4 5.0 collective-permute-start.5
Sparse Core Ops, SparseCore 0:
  10.5 108.3 all-gather.4
  137.4 70.0 all-gather.6
  410.4 67.2 all-gather.8
  680.6 67.2 all-gather.10
where the time goes:
time: 864 us; the launch traced here: 863 us
  blocking collectives  495 us (57%)
  waiting for transfers between devices  260 us (30%)
  local copies, waits for them, and re-layouts  36.3 us (4%)
  starting transfers between devices  26.9 us (3%)
  matrix products  18.3 us (2%)
  between operations  13.5 us (2%)
  other arithmetic  12.5 us (1%)
    psum x3, blocking collectives, squares(): return lax.psum(jnp.sum(residual * residual, axis=1), ('band', 'seq'))  291 us
    psum x2, blocking collectives, on_device(): curve = lax.psum(jnp.sum(direction * image, axis=1), ('band', 'seq'))  204 us
    all_gather x3, waiting for transfers between devices, on_device(): lax.all_gather(lifted, 'band', axis=1, tiled=True)  173 us
    all_gather x1, waiting for transfers between devices, on_device(): gathered = lax.all_gather(embeddings, 'band', axis=0, tiled=True)  78.1 us
  transfers between devices with their start and end apart: 11, of which 7 were waited for; matrix products, arithmetic and copies ran while one was open for 3% of the time, Pallas kernels for 0%

commit v1 on v0

--- a/solution.py
+++ b/solution.py
@@ -92,7 +92,9 @@
         near_term = jnp.einsum(
             "tcw,twa->cta", windows, band_tiles, preferred_element_type=jnp.float32
         ).reshape(channels, frames)
-        spread = lax.all_gather(lifted, "band", axis=1, tiled=True).reshape(channels, -1, 128)
+        spread = jnp.concatenate(
+            lax.all_to_all(jnp.stack([lifted] * lax.axis_size("band")), "band", 0, 0), axis=1
+        ).reshape(channels, -1, 128)
         far_tiles = spread[:, partners]
         far_term = jnp.einsum(
             "ctkj,tkji->cti", far_tiles, affinity, preferred_element_type=jnp.float32

time: 864 us -> 758 us (0.88)
  waiting for transfers between devices: 260 us -> 131 us
  starting transfers between devices: 26.9 us -> 44.4 us
    all_gather x3 -> x0, waiting for transfers between devices: 173 us -> none  [on_device(): lax.all_gather(lifted, 'band', axis=1, tiled=True)]
    all_to_all x0 -> x3, waiting for transfers between devices: none -> 42.5 us  [on_device(): lax.all_to_all(jnp.stack([lifted] * lax.axis_size('band')), 'band', 0, 0)]
    all_to_all x0 -> x3, starting transfers between devices: none -> 17.2 us  [on_device(): lax.all_to_all(jnp.stack([lifted] * lax.axis_size('band')), 'band', 0, 0)]
  transfers between devices with their start and end apart: 11 -> 11, of which waited for: 7 -> 7; matrix products, arithmetic and copies ran while one was open for 3% -> 4% of each run, Pallas kernels for 0% -> 0%
where the time goes in v1:
time: 758 us; the launch traced here: 756 us
  blocking collectives  491 us (65%)
  waiting for transfers between devices  131 us (17%)
  starting transfers between devices  44.4 us (6%)
  local copies, waits for them, and re-layouts  39.3 us (5%)
  matrix products  21.3 us (3%)
  other arithmetic  15.8 us (2%)
  between operations  13.9 us (2%)
    psum x3, blocking collectives, squares(): return lax.psum(jnp.sum(residual * residual, axis=1), ('band', 'seq'))  290 us
    psum x2, blocking collectives, on_device(): curve = lax.psum(jnp.sum(direction * image, axis=1), ('band', 'seq'))  201 us
    all_gather x1, waiting for transfers between devices, on_device(): gathered = lax.all_gather(embeddings, 'band', axis=0, tiled=True)  78.2 us
    all_to_all x3, waiting for transfers between devices, on_device(): lax.all_to_all(jnp.stack([lifted] * lax.axis_size('band')), 'band', 0, 0)  42.5 us
    all_to_all x3, starting transfers between devices, on_device(): lax.all_to_all(jnp.stack([lifted] * lax.axis_size('band')), 'band', 0, 0)  17.2 us
  transfers between devices with their start and end apart: 11, of which 7 were waited for; matrix products, arithmetic and copies ran while one was open for 4% of the time, Pallas kernels for 0%

profile of v1, /device:TPU:1, one launch (start us, length us, event | category | flops | bytes accessed | tf_op | source)
XLA Modules:
  0.0 756.3 jit_solution(10296221404760137009)
XLA Ops:
  6.5 0.7 all-gather.2.cloned.1.call-update
  7.3 0.7 convert_element_type.59
  7.9 0.8 broadcast_multiply_fusion
  9.4 1.3 reduce.11
  10.8 0.7 compare_select_fusion.1
  11.5 1.3 gather_fusion
  13.0 0.8 reshape.600
  13.7 10.5 %all-to-all-start = ((bf16[32,2,256]{2,1,0:T(2,128)(2,1)}), bf16[32,2,256]{2,1,0:T(2,128)(2,1)S(1)}, u32[]{:S(2)}, u32[]{:S(2)}) async-start(bf16[32,2,256]{2,1,0:T(2,128)(2,1)} %reshape.600), calls=%async_computation | async-start | bytes 65536 | tf_op jit(solution)/shard_map/all_to_all | solution.py:39
  24.3 1.0 reduce-window.9
  25.9 4.5 gather_fusion.1
  30.6 2.3 gather_fusion.2
  32.9 6.8 gather_fusion.3
  40.8 78.2 %all-gather.2.cloned.1.call-done = bf16[16384,256]{1,0:T(8,128)(2,1)} async-done(((bf16[512,256]{1,0:T(8,128)(2,1)}), bf16[16384,256]{1,0:T(8,128)(2,1)}) %all-gather.2.cloned.1.call-update) | async-done | bytes 8388624 | tf_op jit(solution)/shard_map/all_gather | solution.py:62
  119.1 10.0 %gather_fusion.4 = bf16[128,128,256]{2,1,0:T(8,128)(2,1)} fusion(bf16[128,128,256]{2,1,0:T(8,128)(2,1)} %bitcast.149, s32[1024]{0:T(1024)S(1)} %pad_clamp_fusion), kind=kCustom, calls=%fused_computation.4 | custom fusion | bytes 16777728 | tf_op jit(solution)/shard_map/gather | solution.py:64
  129.1 7.7 %convert_reduce_fusion = (f32[4,128]{1,0:T(4,128)S(1)}, bf16[4,32,128,128]{3,2,1,0:T(8,128)(2,1)}) fusion(f32[4,32]{1,0:T(4,128)S(1)} %convert_multiply_fusion.3, bf16[4,32,128,256]{3,2,1,0:T(8,128)(2,1)} %bitcast.150, bf16[4,128,256,1]{2,1,3,0:T(8,128)(2,1)S(1)} %bitcast.164), kind=kOutput, calls=%fused_computation.8 | convolution fusion | flops 1086324224 | bytes 12847616 | tf_op jit(solution)/shard_map/tkje,tie->tkji/dot_general | solution.py:66
  136.7 0.6 broadcast_multiply_fusion.1
  137.3 1.1 stack.41
  138.4 5.5 all-to-all-start.1
  144.0 4.5 collective-permute-start
  148.5 1.9 collective-permute-start.1
  150.6 3.2 collective-permute-done.1
  153.9 0.6 fusion.13
  154.5 14.2 %all-to-all-done.1 = bf16[32,32,512]{2,1,0:T(8,128)(2,1)S(1)} async-done(((bf16[32,32,512]{2,1,0:T(8,128)(2,1)}), bf16[32,32,512]{2,1,0:T(8,128)(2,1)S(1)}, u32[]{:S(2)}, u32[]{:S(2)}) %all-to-all-start.1) | async-done | bytes 1048608 | tf_op jit(solution)/shard_map/all_to_all | solution.py:96
  168.7 0.6 copy.62
  169.3 0.7 reshape_reshape.9
  170.0 0.7 copy.63
  170.7 0.8 gather_fusion.5
  171.5 2.9 fusion.3
  174.7 100.9 %all-reduce = (f32[32]{0:T(128)S(1)}, f32[32]{0:T(128)S(1)}) all-reduce(f32[32]{0:T(128)S(1)} %get-tuple-element.6, f32[32]{0:T(128)S(1)} %get-tuple-element.5), channel_id=1, replica_groups=mesh['band'=32,'seq'=16] {'band','seq'}, use_global_device_ids=true, to_apply=%region_1.2 | all-reduce | flops 64 | bytes 512 | tf_op jit(solution)/shard_map/psum | solution.py:79
  275.8 94.4 %psum.44 = f32[32]{0:T(128)S(1)} all-reduce(f32[32]{0:T(128)S(1)} %multiply_reduce_fusion.2), channel_id=1, replica_groups=mesh['band'=32,'seq'=16] {'band','seq'}, use_global_device_ids=true, to_apply=%region_10.11 | all-reduce | flops 32 | bytes 256 | tf_op jit(solution)/shard_map/psum | solution.py:79
  370.2 0.9 multiply_convert_fusion.2
  371.1 1.1 stack.47
  372.2 5.3 all-to-all-start.2
  377.6 3.2 collective-permute-start.2
  380.8 1.9 collective-permute-start.3
  382.7 3.0 collective-permute-done.3
  385.9 2.1 fusion.14
  388.0 14.2 %all-to-all-done.2 = bf16[32,32,512]{2,1,0:T(8,128)(2,1)S(1)} async-done(((bf16[32,32,512]{2,1,0:T(8,128)(2,1)}), bf16[32,32,512]{2,1,0:T(8,128)(2,1)S(1)}, u32[]{:S(2)}, u32[]{:S(2)}) %all-to-all-start.2) | async-done | bytes 1048608 | tf_op jit(solution)/shard_map/all_to_all | solution.py:96
  402.8 0.7 reshape_reshape.10
  403.4 0.7 copy.71
  404.1 0.9 gather_fusion.6
  405.0 2.9 fusion.2
  408.1 0.9 multiply_reduce_fusion.1
  409.0 100.5 %psum.45 = f32[32]{0:T(128)S(1)} all-reduce(f32[32]{0:T(128)S(1)} %multiply_reduce_fusion.1), channel_id=1, replica_groups=mesh['band'=32,'seq'=16] {'band','seq'}, use_global_device_ids=true, to_apply=%region_12.13 | all-reduce | flops 32 | bytes 256 | tf_op jit(solution)/shard_map/psum | solution.py:103
  509.5 0.6 div.45
  510.1 0.9 multiply_reduce_fusion
  511.0 94.4 %psum.46 = f32[32]{0:T(128)S(1)} all-reduce(f32[32]{0:T(128)S(1)} %multiply_reduce_fusion), channel_id=1, replica_groups=mesh['band'=32,'seq'=16] {'band','seq'}, use_global_device_ids=true, to_apply=%region_14.15 | all-reduce | flops 32 | bytes 256 | tf_op jit(solution)/shard_map/psum | solution.py:79
  605.4 0.6 div.46
  606.0 1.6 multiply_convert_fusion.1
  607.6 1.1 stack.53
  608.7 6.4 all-to-all-start.3
  615.1 3.2 collective-permute-start.4
  618.4 1.9 collective-permute-start.5
  620.3 3.0 collective-permute-done.5
  623.5 2.1 fusion.15
  625.6 14.1 %all-to-all-done.3 = bf16[32,32,512]{2,1,0:T(8,128)(2,1)S(1)} async-done(((bf16[32,32,512]{2,1,0:T(8,128)(2,1)}), bf16[32,32,512]{2,1,0:T(8,128)(2,1)S(1)}, u32[]{:S(2)}, u32[]{:S(2)}) %all-to-all-start.3) | async-done | bytes 1048608 | tf_op jit(solution)/shard_map/all_to_all | solution.py:96
  640.3 0.7 reshape_reshape.11
  641.0 0.7 copy.75
  641.6 0.9 gather_fusion.7
  642.5 2.9 fusion.1
  645.6 0.9 fusion.12
  646.6 100.6 %psum.47 = f32[32]{0:T(128)S(1)} all-reduce(f32[32]{0:T(128)S(1)} %fusion.12), channel_id=1, replica_groups=mesh['band'=32,'seq'=16] {'band','seq'}, use_global_device_ids=true, to_apply=%region_16.17 | all-reduce | flops 32 | bytes 256 | tf_op jit(solution)/shard_map/psum | solution.py:103
  747.1 0.7 div.47
  747.8 1.6 multiply_add_fusion
  (94 shorter events, 5.2 us)
Async XLA Ops:
  6.5 33.2 %copy-start.14 = (s32[4,32]{1,0:T(4,128)S(1)}, s32[4,32]{1,0:T(4,128)}, u32[]{:S(2)}) copy-start(s32[4,32]{1,0:T(4,128)} %param.12) | copy-start | bytes 1540
  6.5 34.0 %copy-start.15 = (s32[4,32]{1,0:T(4,128)S(1)}, s32[4,32]{1,0:T(4,128)}, u32[]{:S(2)}) copy-start(s32[4,32]{1,0:T(4,128)} %param.13) | copy-start | bytes 1540
  6.5 112.5 %all-gather.2.cloned.1.call-start = ((), (), s32[]{:S(2)}) async-start(), calls=%async_computation.4 | async-start | bytes 8650752 | tf_op jit(solution)/shard_map/all_gather | solution.py:62
  13.7 26.8 %all-to-all-start = ((bf16[32,2,256]{2,1,0:T(2,128)(2,1)}), bf16[32,2,256]{2,1,0:T(2,128)(2,1)S(1)}, u32[]{:S(2)}, u32[]{:S(2)}) async-start(bf16[32,2,256]{2,1,0:T(2,128)(2,1)} %reshape.600), calls=%async_computation | async-start | bytes 65536 | tf_op jit(solution)/shard_map/all_to_all | solution.py:39
  30.5 123.4 %copy-start.11 = (s32[4,256]{1,0:T(4,128)}, s32[4,256]{1,0:T(4,128)S(1)}, u32[]{:S(2)}) copy-start(s32[4,256]{1,0:T(4,128)S(1)} %eq.17) | copy-start | bytes 12292
  32.9 121.0 %copy-start.16 = (s32[512]{0:T(512)}, s32[512]{0:T(512)S(1)}, u32[]{:S(2)}) copy-start(s32[512]{0:T(512)S(1)} %gather_fusion.2) | copy-start | bytes 6148
  39.7 114.2 %copy-start.17 = (pred[4,256]{1,0:T(4,128)(4,1)}, pred[4,256]{1,0:T(4,128)(4,1)S(1)}, u32[]{:S(2)}) copy-start(pred[4,256]{1,0:T(4,128)(4,1)S(1)} %and.33) | copy-start | bytes 3076
  39.9 114.0 %copy-start.13 = (s32[4,128]{1,0:T(4,128)}, s32[4,128]{1,0:T(4,128)S(1)}, u32[]{:S(2)}) copy-start(s32[4,128]{1,0:T(4,128)S(1)} %iota_add_fusion.2) | copy-start | bytes 6148
  40.0 114.0 %copy-start.10 = (s32[4,256]{1,0:T(4,128)}, s32[4,256]{1,0:T(4,128)S(1)}, u32[]{:S(2)}) copy-start(s32[4,256]{1,0:T(4,128)S(1)} %iota_add_fusion.1) | copy-start | bytes 12292
  40.6 130.1 %copy-start.5 = (s32[1024]{0:T(1024)}, s32[1024]{0:T(1024)S(1)}, u32[]{:S(2)}) copy-start(s32[1024]{0:T(1024)S(1)} %pad_clamp_fusion) | copy-start | bytes 12292
  40.8 96.5 %copy-start.3 = (f32[32,512]{1,0:T(8,128)}, f32[32,512]{1,0:T(8,128)S(1)}, u32[]{:S(2)}) copy-start(f32[32,512]{1,0:T(8,128)S(1)} %copy.61) | copy-start | bytes 196612
  119.1 10.0 %copy-start.4 = (bf16[512,256]{1,0:T(8,128)(2,1)S(1)}, bf16[512,256]{1,0:T(8,128)(2,1)}, u32[]{:S(2)}) copy-start(bf16[512,256]{1,0:T(8,128)(2,1)} %param.11) | copy-start | bytes 786436
  137.3 37.1 %copy-start.6 = (f32[512]{0:T(512)}, f32[512]{0:T(512)S(1)}, u32[]{:S(2)}) copy-start(f32[512]{0:T(512)S(1)} %get-tuple-element.12) | copy-start | bytes 6148
  138.4 30.3 %all-to-all-start.1 = ((bf16[32,32,512]{2,1,0:T(8,128)(2,1)}), bf16[32,32,512]{2,1,0:T(8,128)(2,1)S(1)}, u32[]{:S(2)}, u32[]{:S(2)}) async-start(bf16[32,32,512]{2,1,0:T(8,128)(2,1)} %stack.41), calls=%async_computation.1 | async-start | bytes 2097152 | tf_op jit(solution)/shard_map/all_to_all | solution.py:96
  144.0 6.5 collective-permute-start
  148.5 5.3 collective-permute-start.1
  174.4 197.8 %copy-start.2 = (f32[4,128,32]{1,2,0:T(8,128)}, f32[4,128,32]{1,2,0:T(8,128)S(1)}, u32[]{:S(2)}) copy-start(f32[4,128,32]{1,2,0:T(8,128)S(1)} %fusion.3) | copy-start | bytes 196612
  275.6 96.6 %copy-start.7 = (f32[32]{0:T(128)}, f32[32]{0:T(128)S(1)}, u32[]{:S(2)}) copy-start(f32[32]{0:T(128)S(1)} %div.43) | copy-start | bytes 388
  370.2 2.0 copy-start.19
  370.2 2.0 copy-start.8
  372.2 29.9 %all-to-all-start.2 = ((bf16[32,32,512]{2,1,0:T(8,128)(2,1)}), bf16[32,32,512]{2,1,0:T(8,128)(2,1)S(1)}, u32[]{:S(2)}, u32[]{:S(2)}) async-start(bf16[32,32,512]{2,1,0:T(8,128)(2,1)} %stack.47), calls=%async_computation.2 | async-start | bytes 2097152 | tf_op jit(solution)/shard_map/all_to_all | solution.py:96
  377.6 5.1 collective-permute-start.2
  380.8 5.0 collective-permute-start.3
  408.1 200.6 %copy-start = (f32[32,4,128]{0,2,1:T(8,128)}, f32[32,4,128]{0,2,1:T(8,128)S(1)}, u32[]{:S(2)}) copy-start(f32[32,4,128]{0,2,1:T(8,128)S(1)} %copy.72) | copy-start | bytes 196612
  510.1 98.6 %copy-start.9 = (f32[32]{0:T(128)}, f32[32]{0:T(128)S(1)}, u32[]{:S(2)}) copy-start(f32[32]{0:T(128)S(1)} %div.45) | copy-start | bytes 388
  605.4 3.3 copy-start.18
  606.0 2.7 copy-start.12
  608.7 31.0 %all-to-all-start.3 = ((bf16[32,32,512]{2,1,0:T(8,128)(2,1)}), bf16[32,32,512]{2,1,0:T(8,128)(2,1)S(1)}, u32[]{:S(2)}, u32[]{:S(2)}) async-start(bf16[32,32,512]{2,1,0:T(8,128)(2,1)} %stack.53), calls=%async_computation.3 | async-start | bytes 2097152 | tf_op jit(solution)/shard_map/all_to_all | solution.py:96
  615.1 5.2 collective-permute-start.4
  618.4 5.0 collective-permute-start.5
  640.9 4.7 copy-start.1
Sparse Core Ops, SparseCore 0:
  10.5 108.4 all-gather.1
